TPU v7x, 32 devices: a whole 2x2x4 slice. The times are simulated.
32 devices in a mesh: dp: 8 (over z, y), feat: 4 (over x, core).
Axes of the slice: x: 2, y: 2, z: 4, core: 2. Of those that a mesh axis runs over, the one named last changes fastest.
Arguments:
- activations: bfloat16 [16384, 2048], P('feat', 'dp'), may hold values from -6 to 6
- cotangent: bfloat16 [16384, 2048], P('feat', 'dp'), may hold values from -6 to 6
- r_mix: bfloat16 [64, 256, 256], P('feat', 'dp'), may hold values from -0.375 to 0.375
- l_mix: bfloat16 [256, 4096], P('feat', 'dp'), may hold values from -0.75 to 0.75
Outputs:
- grad_x: bfloat16 [16384, 2048], P('feat', 'dp')
- grad_r: float32 [64, 256, 256], P('feat', 'dp')
- grad_l: float32 [256, 4096], P('feat', 'dp')
All inputs are finite; a program needn't handle non-finite values.
Results may differ from a plain program's by a relative error of at most 0.0055.
Values may be sent and summed in bfloat16 or wider, within the bound.
No kernel may reach another device: no remote copies, remote signals or barrier semaphores. Data moves between devices by JAX's collectives and lax.ppermute only.
A program may use at most 64 MiB of HBM per device.

v0:
```python
import math
import jax
import jax.numpy as jnp
from jax import lax
from jax.sharding import PartitionSpec as P

BLOCKS = 64
WIDTH = 256


def gelu_tanh(values):
    return jax.nn.gelu(values, approximate=True)


def slope_of(pre_act, upstream):
    _, pullback = jax.vjp(gelu_tanh, pre_act)
    return pullback(upstream.astype(jnp.float32))[0].astype(jnp.bfloat16)


def body(activations, cotangent, r_mix, l_mix):
    tok_count = activations.shape[1]
    local_blocks = activations.shape[0] // WIDTH
    grad_scale = 1.0 / math.sqrt(tok_count * lax.axis_size("dp"))
    r_whole, l_whole = (
        lax.all_gather(r_mix, "dp", axis=1, tiled=True),
        lax.all_gather(l_mix, "dp", axis=1, tiled=True),
    )
    local_cols = l_whole.shape[0]
    l_blocks = l_whole.reshape(local_cols, BLOCKS, BLOCKS)
    x_blocks = activations.reshape(local_blocks, WIDTH, tok_count)
    g_blocks = cotangent.reshape(local_blocks, WIDTH, tok_count)
    mixed_rows = jnp.einsum(
        "bit,bio->bot", x_blocks, r_whole, preferred_element_type=jnp.float32
    ).astype(jnp.bfloat16)
    outgoing = (mixed_rows,)
    parts = (lax.all_to_all(outgoing[0], "feat", split_axis=1, concat_axis=0, tiled=True),)
    columns = parts[0]
    pre_act = jnp.einsum("bst,sbc->cst", columns, l_blocks, preferred_element_type=jnp.float32)
    arrived = (columns, pre_act) + tuple(parts[1:])
    columns = arrived[0]
    pre_act = arrived[1]
    pre_rows = lax.all_to_all(pre_act, "feat", split_axis=0, concat_axis=1, tiled=True)
    slope_rows = slope_of(pre_rows, g_blocks)
    slope_cols = lax.all_to_all(slope_rows, "feat", split_axis=1, concat_axis=0, tiled=True)
    back_cols = jnp.einsum(
        "cst,sbc->bst", slope_cols, l_blocks, preferred_element_type=jnp.float32
    ).astype(jnp.bfloat16)
    l_term = jnp.einsum("bst,cst->sbc", columns, slope_cols, preferred_element_type=jnp.float32)
    l_term = l_term.reshape(local_cols, BLOCKS * BLOCKS) * grad_scale
    back_rows = lax.all_to_all(back_cols, "feat", split_axis=0, concat_axis=1, tiled=True)
    back_rows, through_r = (
        back_rows,
        jnp.einsum("bot,bio->bit", back_rows, r_whole, preferred_element_type=jnp.float32),
    )
    grad_x = (
        (g_blocks.astype(jnp.float32) + through_r)
        .astype(jnp.bfloat16)
        .reshape(local_blocks * WIDTH, tok_count)
    )
    r_term = (
        jnp.einsum("bit,bot->bio", x_blocks, back_rows, preferred_element_type=jnp.float32)
        * grad_scale
    )
    grad_l, grad_r = (
        lax.psum_scatter(l_term, "dp", scatter_dimension=1, tiled=True),
        lax.psum_scatter(r_term, "dp", scatter_dimension=1, tiled=True),
    )
    return (grad_x, grad_r, grad_l)


def solution(mesh):
    placed = (P("feat", "dp"), P("feat", "dp"), P("feat", "dp", None), P("feat", "dp"))
    return jax.shard_map(
        body,
        mesh=mesh,
        in_specs=placed,
        out_specs=(P("feat", "dp"), P("feat", "dp", None), P("feat", "dp")),
        check_vma=False,
    )
```

profile of v0, /device:TPU:0, one launch (start us, length us, event | category | flops | bytes accessed | tf_op | source)
XLA Modules:
  0.0 399.9 jit_solution(9625601833998472881)
XLA Ops:
  7.2 0.7 all-gather.2.cloned.1.call-update
  7.9 54.3 %all-gather.2.cloned.1.call-done = bf16[16,256,256]{2,1,0:T(8,128)(2,1)} async-done(((bf16[16,32,256]{2,1,0:T(8,128)(2,1)}), bf16[16,256,256]{2,1,0:T(8,128)(2,1)}) %all-gather.2.cloned.1.call-update) | async-done | bytes 2097168 | tf_op jit(solution)/shard_map/all_gather | solution.py:25
  62.2 2.4 convolution_convert_fusion
  64.6 2.5 copy.19
  67.1 4.6 %all-to-all-start = ((bf16[16,256,256]{2,0,1:T(8,128)(2,1)}), bf16[16,256,256]{2,0,1:T(8,128)(2,1)}, u32[]{:S(2)}, u32[]{:S(2)}) async-start(bf16[16,256,256]{2,0,1:T(8,128)(2,1)} %copy.19), calls=%async_computation | async-start | bytes 4194304 | tf_op jit(solution)/shard_map/all_to_all | solution.py:36
  71.7 33.3 %all_gather.7 = bf16[64,4096]{1,0:T(8,128)(2,1)} all-gather(bf16[64,512]{1,0:T(8,128)(2,1)S(1)} %copy-done.5), channel_id=1, replica_groups=mesh['dp'=8,'feat'=4] {'dp'}, dimensions={1}, use_global_device_ids=true | all-gather | bytes 589824 | tf_op jit(solution)/shard_map/all_gather | solution.py:26
  105.0 2.1 reshape.22
  107.1 1.8 copy.20
  109.0 1.3 copy-done.1
  110.3 0.8 convolution_bitcast_fusion
  111.0 2.4 copy.22
  113.5 51.1 %all_to_all.72 = f32[64,64,256]{2,1,0:T(8,128)S(1)} all-to-all(f32[64,64,256]{2,1,0:T(8,128)S(1)} %copy.22), channel_id=1, replica_groups=mesh['dp'=8,'feat'=4] {'feat'}, dimensions={0} | all-to-all | bytes 8388608 | tf_op jit(solution)/shard_map/all_to_all | solution.py:42
  164.6 0.5 copy.23
  165.0 1.1 copy-done.4
  166.1 3.3 fusion.6
  169.5 1.2 copy.24
  170.6 28.2 %all_to_all.73 = bf16[16,256,256]{2,0,1:T(8,128)(2,1)S(1)} all-to-all(bf16[16,256,256]{2,0,1:T(8,128)(2,1)S(1)} %copy.24), channel_id=1, replica_groups=mesh['dp'=8,'feat'=4] {'feat'}, dimensions={1} | all-to-all | bytes 4194304 | tf_op jit(solution)/shard_map/all_to_all | solution.py:44
  198.8 0.3 copy.25
  199.1 0.7 convert_bitcast_fusion
  199.8 0.6 copy-done.2
  200.4 1.2 copy.26
  201.6 28.2 %all_to_all.74 = bf16[64,64,256]{2,1,0:T(8,128)(2,1)S(1)} all-to-all(bf16[64,64,256]{2,1,0:T(8,128)(2,1)S(1)} %copy.26), channel_id=1, replica_groups=mesh['dp'=8,'feat'=4] {'feat'}, dimensions={0} | all-to-all | bytes 4194304 | tf_op jit(solution)/shard_map/all_to_all | solution.py:50
  229.8 0.2 copy.27
  230.0 1.3 copy-done.3
  231.4 2.7 multiply_bitcast_fusion
  234.1 5.5 %copy.28 = f32[16,256,256]{2,0,1:T(8,128)} copy(f32[16,256,256]{1,2,0:T(8,128)} %multiply_bitcast_fusion) | data formatting | bytes 8388608 | tf_op jit(solution)/shard_map/mul | solution.py:61
  239.6 4.2 %convolution_multiply_fusion = f32[64,64,64]{2,1,0:T(8,128)} fusion(bf16[64,64,256]{2,0,1:T(8,128)(2,1)} %bitcast.50, bf16[64,64,256]{2,0,1:T(8,128)(2,1)} %bitcast.52), kind=kOutput, calls=%fused_computation.20 | convolution fusion | flops 134479872 | bytes 5242880 | tf_op jit(solution)/shard_map/bst,cst->sbc/dot_general | solution.py:48
  243.9 3.1 mul.78
  247.0 4.9 %fusion.10 = bf16[16,256,256]{2,1,0:T(8,128)(2,1)} fusion(bf16[16,256,256]{2,1,0:T(8,128)(2,1)} %bitcast.58, bf16[16,256,256]{2,1,0:T(8,128)(2,1)} %all-gather.2.cloned.1.call-done, bf16[16,256,256]{2,1,0:T(8,128)(2,1)} %bitcast.54), kind=kOutput, calls=%fused_computation.15 | convolution fusion | flops 540016640 | bytes 8388608 | tf_op jit(solution)/shard_map/bot,bio->bit/dot_general | solution.py:53
  251.9 73.5 %reduce-scatter.3.cloned.1.call-done = f32[16,32,256]{2,0,1:T(8,128)} async-done(((f32[16,256,256]{2,0,1:T(8,128)}), f32[16,32,256]{2,0,1:T(8,128)}) %reduce-scatter.3.cloned.1.call-update) | async-done | bytes 524304 | tf_op jit(solution)/shard_map/reduce_scatter | solution.py:66
  325.4 2.1 copy.29
  327.6 65.8 %reduce-scatter.5.cloned.1.call-done = f32[64,512]{1,0:T(8,128)} async-done(((f32[64,4096]{1,0:T(8,128)}), f32[64,512]{1,0:T(8,128)}) %reduce-scatter.5.cloned.1.call-update) | async-done | bytes 131088 | tf_op jit(solution)/shard_map/reduce_scatter | solution.py:65
  (14 shorter events, 0.2 us)
Async XLA Ops:
  7.2 55.0 %copy-start = (bf16[4096,256]{1,0:T(8,128)(2,1)S(1)}, bf16[4096,256]{1,0:T(8,128)(2,1)}, u32[]{:S(2)}) copy-start(bf16[4096,256]{1,0:T(8,128)(2,1)} %param.4) | copy-start | bytes 6291460
  7.2 55.0 %all-gather.2.cloned.1.call-start = ((), (), s32[]{:S(2)}) async-start(), calls=%async_computation.6 | async-start | bytes 2359296 | tf_op jit(solution)/shard_map/all_gather | solution.py:25
  67.1 4.6 %copy-start.5 = (bf16[64,512]{1,0:T(8,128)(2,1)S(1)}, bf16[64,512]{1,0:T(8,128)(2,1)}, u32[]{:S(2)}) copy-start(bf16[64,512]{1,0:T(8,128)(2,1)} %param.7) | copy-start | bytes 196612
  67.1 40.0 %all-to-all-start = ((bf16[16,256,256]{2,0,1:T(8,128)(2,1)}), bf16[16,256,256]{2,0,1:T(8,128)(2,1)}, u32[]{:S(2)}, u32[]{:S(2)}) async-start(bf16[16,256,256]{2,0,1:T(8,128)(2,1)} %copy.19), calls=%async_computation | async-start | bytes 4194304 | tf_op jit(solution)/shard_map/all_to_all | solution.py:36
  71.6 253.8 %reduce-scatter.3.cloned.1.call-start = ((), (), s32[]{:S(2)}) async-start(), calls=%async_computation.7 | async-start | bytes 4718592 | tf_op jit(solution)/shard_map/reduce_scatter | solution.py:66
  109.0 1.3 copy-start.1
  164.6 1.6 copy-start.4
  199.1 1.3 copy-start.2
  230.0 1.3 copy-start.3
  239.6 153.8 %reduce-scatter.5.cloned.1.call-start = ((), (), s32[]{:S(2)}) async-start(), calls=%async_computation.8 | async-start | bytes 1179648 | tf_op jit(solution)/shard_map/reduce_scatter | solution.py:65
Sparse Core Ops, SparseCore 0:
  10.2 51.9 all-gather.1
  239.7 85.6 reduce-scatter.2
  329.8 63.5 reduce-scatter.4
where the time goes:
time: 401 us; the launch traced here: 400 us
  waiting for transfers between devices  194 us (48%)
  blocking collectives  141 us (35%)
  local copies, waits for them, and re-layouts  27.3 us (7%)
  matrix products  15.7 us (4%)
  between operations  13.9 us (3%)
  starting transfers between devices  4.69 us (1%)
    reduce_scatter x1, waiting for transfers between devices, body(): lax.psum_scatter(r_term, 'dp', scatter_dimension=1, tiled=True)  73.5 us
    reduce_scatter x1, waiting for transfers between devices, body(): lax.psum_scatter(l_term, 'dp', scatter_dimension=1, tiled=True)  65.8 us
    all_gather x1, waiting for transfers between devices, body(): lax.all_gather(r_mix, 'dp', axis=1, tiled=True)  54.3 us
    all_to_all x1, blocking collectives, body(): lax.all_to_all(pre_act, 'feat', split_axis=0, concat_axis=1, tiled=True)  51.1 us
    all_gather x1, blocking collectives, body(): lax.all_gather(l_mix, 'dp', axis=1, tiled=True)  33.3 us
    all_to_all x1, blocking collectives, body(): lax.all_to_all(slope_rows, 'feat', split_axis=1, concat_axis=0, tiled=True)  28.2 us
    all_to_all x1, blocking collectives, body(): lax.all_to_all(back_cols, 'feat', split_axis=0, concat_axis=1, tiled=True)  28.2 us
  transfers between devices with their start and end apart: 4, of which 3 were waited for; matrix products, arithmetic and copies ran while one was open for 4% of the time, Pallas kernels for 0%

commit v1 on v0

--- a/solution.py
+++ b/solution.py
@@ -6,6 +6,28 @@
 
 BLOCKS = 64
 WIDTH = 256
+
+
+def in_blocks(shard, dim, length):
+    before, after = (shard.shape[:dim], shard.shape[dim + 1 :])
+    return jnp.moveaxis(shard.reshape(*before, length, -1, *after), dim, 0)
+
+
+def in_order(pieces, dim):
+    lengths = list(pieces.shape[1:])
+    lengths[dim] *= pieces.shape[0]
+    return jnp.moveaxis(pieces, 0, dim).reshape(lengths)
+
+
+def pairwise_exchange(x, axis, split_dim, concat_dim):
+    count, position = (lax.axis_size(axis), lax.axis_index(axis))
+    tiles = in_blocks(x, split_dim, count)
+    finished = [tiles[position]]
+    for turn in range(1, count):
+        sent = tiles[position ^ turn]
+        finished.append(lax.ppermute(sent, axis, [(i, i ^ turn) for i in range(count)]))
+    tiles = jnp.stack(finished)[position ^ jnp.arange(count)]
+    return in_order(tiles, concat_dim)
 
 
 def gelu_tanh(values):
@@ -39,7 +61,7 @@
     arrived = (columns, pre_act) + tuple(parts[1:])
     columns = arrived[0]
     pre_act = arrived[1]
-    pre_rows = lax.all_to_all(pre_act, "feat", split_axis=0, concat_axis=1, tiled=True)
+    pre_rows = pairwise_exchange(pre_act, "feat", 0, 1)
     slope_rows = slope_of(pre_rows, g_blocks)
     slope_cols = lax.all_to_all(slope_rows, "feat", split_axis=1, concat_axis=0, tiled=True)
     back_cols = jnp.einsum(

time: 401 us -> 406 us (1.012)
  blocking collectives: 141 us -> 89.7 us
  waiting for transfers between devices: 194 us -> 240 us
  local copies, waits for them, and re-layouts: 27.3 us -> 32.9 us
    all_to_all x1 -> x0, blocking collectives: 51.1 us -> none  [body(): lax.all_to_all(pre_act, 'feat', split_axis=0, concat_axis=1, tiled=True)]
    ppermute x0 -> x3, waiting for transfers between devices: none -> 46 us  [pairwise_exchange(): lax.ppermute(sent, axis, [(i, i ^ turn) for i in range(count)])]
    gather x0 -> x1, local copies, waits for them, and re-layouts: none -> 4.97 us  [pairwise_exchange(): tiles = jnp.stack(finished)[position ^ jnp.arange(count)]]
  transfers between devices with their start and end apart: 4 -> 7, of which waited for: 3 -> 5; matrix products, arithmetic and copies ran while one was open for 4% -> 4% of each run, Pallas kernels for 0% -> 0%
where the time goes in v1:
time: 406 us; the launch traced here: 405 us
  waiting for transfers between devices  240 us (59%)
  blocking collectives  89.7 us (22%)
  local copies, waits for them, and re-layouts  32.9 us (8%)
  matrix products  15.7 us (4%)
  between operations  13.9 us (3%)
  starting transfers between devices  6.69 us (2%)
  other arithmetic  5.91 us (1%)
    reduce_scatter x1, waiting for transfers between devices, body(): lax.psum_scatter(r_term, 'dp', scatter_dimension=1, tiled=True)  73.6 us
    reduce_scatter x1, waiting for transfers between devices, body(): lax.psum_scatter(l_term, 'dp', scatter_dimension=1, tiled=True)  65.9 us
    all_gather x1, waiting for transfers between devices, body(): lax.all_gather(r_mix, 'dp', axis=1, tiled=True)  54.3 us
    ppermute x3, waiting for transfers between devices, pairwise_exchange(): lax.ppermute(sent, axis, [(i, i ^ turn) for i in range(count)])  46 us
    all_gather x1, blocking collectives, body(): lax.all_gather(l_mix, 'dp', axis=1, tiled=True)  33.3 us
    all_to_all x1, blocking collectives, body(): lax.all_to_all(slope_rows, 'feat', split_axis=1, concat_axis=0, tiled=True)  28.2 us
    all_to_all x1, blocking collectives, body(): lax.all_to_all(back_cols, 'feat', split_axis=0, concat_axis=1, tiled=True)  28.2 us
  transfers between devices with their start and end apart: 7, of which 5 were waited for; matrix products, arithmetic and copies ran while one was open for 4% of the time, Pallas kernels for 0%

profile of v1, /device:TPU:0, one launch (start us, length us, event | category | flops | bytes accessed | tf_op | source)
XLA Modules:
  0.0 405.2 jit_solution(717810089733160234)
XLA Ops:
  7.2 0.7 all-gather.2.cloned.1.call-update
  7.9 54.3 %all-gather.2.cloned.1.call-done = bf16[16,256,256]{2,1,0:T(8,128)(2,1)} async-done(((bf16[16,32,256]{2,1,0:T(8,128)(2,1)}), bf16[16,256,256]{2,1,0:T(8,128)(2,1)}) %all-gather.2.cloned.1.call-update) | async-done | bytes 2097168 | tf_op jit(solution)/shard_map/all_gather | solution.py:47
  62.2 2.4 convolution_convert_fusion
  64.6 2.5 copy.19
  67.1 4.6 %all-to-all-start = ((bf16[16,256,256]{2,0,1:T(8,128)(2,1)}), bf16[16,256,256]{2,0,1:T(8,128)(2,1)}, u32[]{:S(2)}, u32[]{:S(2)}) async-start(bf16[16,256,256]{2,0,1:T(8,128)(2,1)} %copy.19), calls=%async_computation | async-start | bytes 4194304 | tf_op jit(solution)/shard_map/all_to_all | solution.py:58
  71.7 33.3 %all_gather.7 = bf16[64,4096]{1,0:T(8,128)(2,1)} all-gather(bf16[64,512]{1,0:T(8,128)(2,1)S(1)} %copy-done.5), channel_id=1, replica_groups=mesh['dp'=8,'feat'=4] {'dp'}, dimensions={1}, use_global_device_ids=true | all-gather | bytes 589824 | tf_op jit(solution)/shard_map/all_gather | solution.py:48
  105.0 2.1 reshape.44
  107.1 1.8 copy.20
  109.0 0.8 fusion.12
  110.3 0.6 constant_dynamic-slice_fusion
  111.0 1.9 collective-permute-start.1
  112.9 23.2 %collective-permute-done.2 = f32[16,64,256]{2,0,1:T(8,128)S(1)} collective-permute-done((f32[16,64,256]{2,0,1:T(8,128)S(1)}, f32[16,64,256]{2,0,1:T(8,128)S(1)}, u32[]{:S(2)}, u32[]{:S(2)}) %collective-permute-start.2) | collective-permute-done | bytes 1048608 | tf_op jit(solution)/shard_map/ppermute | solution.py:28
  136.1 22.8 %collective-permute-done.1 = f32[16,64,256]{2,0,1:T(8,128)S(1)} collective-permute-done((f32[16,64,256]{2,0,1:T(8,128)S(1)}, f32[16,64,256]{2,0,1:T(8,128)S(1)}, u32[]{:S(2)}, u32[]{:S(2)}) %collective-permute-start.1) | collective-permute-done | bytes 1048608 | tf_op jit(solution)/shard_map/ppermute | solution.py:28
  158.9 2.6 pad_maximum_fusion
  161.5 5.0 %gather_fusion = f32[4,16,64,256]{3,1,2,0:T(8,128)} fusion(f32[4,16,64,256]{3,1,0,2:T(8,128)} %pad_maximum_fusion, s32[1024]{0:T(1024)S(1)} %pad_clamp_fusion), kind=kCustom, calls=%fused_computation | custom fusion | bytes 8388624 | tf_op jit(solution)/shard_map/gather | solution.py:29
  166.4 4.8 %copy.22 = f32[16,4,64,256]{3,2,1,0:T(8,128)S(1)} copy(f32[16,4,64,256]{3,0,2,1:T(8,128)} %bitcast.66) | data formatting | bytes 8388608 | tf_op jit(solution)/shard_map/transpose | solution.py:19
  171.2 3.3 fusion.6
  174.5 1.2 copy.23
  175.7 28.2 %all_to_all.54 = bf16[16,256,256]{2,0,1:T(8,128)(2,1)S(1)} all-to-all(bf16[16,256,256]{2,0,1:T(8,128)(2,1)S(1)} %copy.23), channel_id=1, replica_groups=mesh['dp'=8,'feat'=4] {'feat'}, dimensions={1} | all-to-all | bytes 4194304 | tf_op jit(solution)/shard_map/all_to_all | solution.py:66
  204.2 0.7 convert_bitcast_fusion
  204.9 0.6 copy-done.2
  205.5 1.2 copy.25
  206.7 28.2 %all_to_all.55 = bf16[64,64,256]{2,1,0:T(8,128)(2,1)S(1)} all-to-all(bf16[64,64,256]{2,1,0:T(8,128)(2,1)S(1)} %copy.25), channel_id=1, replica_groups=mesh['dp'=8,'feat'=4] {'feat'}, dimensions={0} | all-to-all | bytes 4194304 | tf_op jit(solution)/shard_map/all_to_all | solution.py:72
  235.2 1.3 copy-done.3
  236.5 2.7 multiply_bitcast_fusion
  239.2 5.5 %copy.27 = f32[16,256,256]{2,0,1:T(8,128)} copy(f32[16,256,256]{1,2,0:T(8,128)} %multiply_bitcast_fusion) | data formatting | bytes 8388608 | tf_op jit(solution)/shard_map/mul | solution.py:83
  244.8 4.3 %convolution_multiply_fusion = f32[64,64,64]{2,1,0:T(8,128)} fusion(bf16[64,64,256]{2,0,1:T(8,128)(2,1)} %bitcast.60, bf16[64,64,256]{2,0,1:T(8,128)(2,1)} %bitcast.62), kind=kOutput, calls=%fused_computation.21 | convolution fusion | flops 134479872 | bytes 5242880 | tf_op jit(solution)/shard_map/bst,cst->sbc/dot_general | solution.py:70
  249.0 3.2 mul.78
  252.2 4.9 %fusion.10 = bf16[16,256,256]{2,1,0:T(8,128)(2,1)} fusion(bf16[16,256,256]{2,1,0:T(8,128)(2,1)} %bitcast.69, bf16[16,256,256]{2,1,0:T(8,128)(2,1)} %all-gather.2.cloned.1.call-done, bf16[16,256,256]{2,1,0:T(8,128)(2,1)} %bitcast.64), kind=kOutput, calls=%fused_computation.16 | convolution fusion | flops 540016640 | bytes 8388608 | tf_op jit(solution)/shard_map/bot,bio->bit/dot_general | solution.py:75
  257.1 73.6 %reduce-scatter.3.cloned.1.call-done = f32[16,32,256]{2,0,1:T(8,128)} async-done(((f32[16,256,256]{2,0,1:T(8,128)}), f32[16,32,256]{2,0,1:T(8,128)}) %reduce-scatter.3.cloned.1.call-update) | async-done | bytes 524304 | tf_op jit(solution)/shard_map/reduce_scatter | solution.py:88
  330.7 2.1 copy.28
  332.9 65.9 %reduce-scatter.5.cloned.1.call-done = f32[64,512]{1,0:T(8,128)} async-done(((f32[64,4096]{1,0:T(8,128)}), f32[64,512]{1,0:T(8,128)}) %reduce-scatter.5.cloned.1.call-update) | async-done | bytes 131088 | tf_op jit(solution)/shard_map/reduce_scatter | solution.py:87
  (23 shorter events, 1.4 us)
Async XLA Ops:
  7.2 55.0 %copy-start = (bf16[4096,256]{1,0:T(8,128)(2,1)S(1)}, bf16[4096,256]{1,0:T(8,128)(2,1)}, u32[]{:S(2)}) copy-start(bf16[4096,256]{1,0:T(8,128)(2,1)} %param.4) | copy-start | bytes 6291460
  7.2 55.0 %all-gather.2.cloned.1.call-start = ((), (), s32[]{:S(2)}) async-start(), calls=%async_computation.5 | async-start | bytes 2359296 | tf_op jit(solution)/shard_map/all_gather | solution.py:47
  67.1 4.7 %copy-start.5 = (bf16[64,512]{1,0:T(8,128)(2,1)S(1)}, bf16[64,512]{1,0:T(8,128)(2,1)}, u32[]{:S(2)}) copy-start(bf16[64,512]{1,0:T(8,128)(2,1)} %param.7) | copy-start | bytes 196612
  67.1 40.1 %all-to-all-start = ((bf16[16,256,256]{2,0,1:T(8,128)(2,1)}), bf16[16,256,256]{2,0,1:T(8,128)(2,1)}, u32[]{:S(2)}, u32[]{:S(2)}) async-start(bf16[16,256,256]{2,0,1:T(8,128)(2,1)} %copy.19), calls=%async_computation | async-start | bytes 4194304 | tf_op jit(solution)/shard_map/all_to_all | solution.py:58
  71.6 259.1 %reduce-scatter.3.cloned.1.call-start = ((), (), s32[]{:S(2)}) async-start(), calls=%async_computation.6 | async-start | bytes 4718592 | tf_op jit(solution)/shard_map/reduce_scatter | solution.py:88
  109.0 1.3 copy-start.1
  110.9 25.2 %collective-permute-start.2 = (f32[16,64,256]{2,0,1:T(8,128)S(1)}, f32[16,64,256]{2,0,1:T(8,128)S(1)}, u32[]{:S(2)}, u32[]{:S(2)}) collective-permute-start(f32[16,64,256]{2,0,1:T(8,128)S(1)} %get-tuple-element.13), channel_id=1, source_target_pairs={{0,3},{1,2},{2,1},{3,0},{4,7},{5,6},{6,5},{7,4},{8,11},{9,10},{10,... | collective-permute-start | bytes 3145736 | tf_op jit(solution)/shard_map/ppermute | solution.py:28
  111.0 47.9 %collective-permute-start.1 = (f32[16,64,256]{2,0,1:T(8,128)S(1)}, f32[16,64,256]{2,0,1:T(8,128)S(1)}, u32[]{:S(2)}, u32[]{:S(2)}) collective-permute-start(f32[16,64,256]{2,0,1:T(8,128)S(1)} %get-tuple-element.14), channel_id=1, source_target_pairs={{0,2},{1,3},{2,0},{3,1},{4,6},{5,7},{6,4},{7,5},{8,10},{9,11},{10,... | collective-permute-start | bytes 3145736 | tf_op jit(solution)/shard_map/ppermute | solution.py:28
  112.9 46.0 %collective-permute-start = (f32[16,64,256]{2,0,1:T(8,128)S(1)}, f32[16,64,256]{2,0,1:T(8,128)S(1)}, u32[]{:S(2)}, u32[]{:S(2)}) collective-permute-start(f32[16,64,256]{2,0,1:T(8,128)S(1)} %get-tuple-element.15), channel_id=1, source_target_pairs={{0,1},{1,0},{2,3},{3,2},{4,5},{5,4},{6,7},{7,6},{8,9},{9,8},{10,11... | collective-permute-start | bytes 3145736 | tf_op jit(solution)/shard_map/ppermute | solution.py:28
  166.4 4.8 %copy-start.4 = (bf16[4096,256]{1,0:T(8,128)(2,1)S(1)}, bf16[4096,256]{1,0:T(8,128)(2,1)}, u32[]{:S(2)}) copy-start(bf16[4096,256]{1,0:T(8,128)(2,1)} %param.5) | copy-start | bytes 6291460
  204.2 1.3 copy-start.2
  235.1 1.3 copy-start.3
  244.7 154.0 %reduce-scatter.5.cloned.1.call-start = ((), (), s32[]{:S(2)}) async-start(), calls=%async_computation.7 | async-start | bytes 1179648 | tf_op jit(solution)/shard_map/reduce_scatter | solution.py:87
Sparse Core Ops, SparseCore 0:
  10.2 51.9 all-gather.1
  244.8 85.8 reduce-scatter.2
  335.1 63.5 reduce-scatter.4
